TPU v7x, 128 devices: a whole 4x4x4 slice. The times are simulated.
128 devices in a mesh: lat: 32 (over x, y, core), dep: 4 (over z).
Axes of the slice: x: 4, y: 4, z: 4, core: 2. Of those that a mesh axis runs over, the one named last changes fastest.
Arguments:
- spectrum: float32 [4, 512, 2, 32768], P('dep', 'lat'), may hold values from -6 to 6
- operator: float32 [2, 2048, 2048], P(None, None, 'dep'), may hold values from -0.125 to 0.125
- pattern: int32 [2, 16, 16], replicated, may hold values 0 or 1
- band: int32 [32768], P('lat'), may hold values from 0 to 1
Outputs:
- blurred: float32 [2048, 2, 32768], P('dep', None, 'lat')
All inputs are finite; a program needn't handle non-finite values.
Results may differ from a plain program's by a relative error of at most 0.0001.
Values sent between devices are 32-bit elements; how exact they have to be, the bound alone decides.
No kernel may reach another device: no remote copies, remote signals or barrier semaphores. Data moves between devices by JAX's collectives and lax.ppermute only.
A program may use at most 128 MiB of HBM per device.

v0:
```python
import jax
import jax.numpy as jnp
from jax import lax
from jax.sharding import PartitionSpec as P

BLOCK = 128


def apply_pattern(weights, blocks):
    bands_count, out_size, in_size = weights.shape
    shaped = weights.reshape(bands_count, out_size // BLOCK, BLOCK, in_size // BLOCK, BLOCK)
    factor = blocks.astype(jnp.float32)[:, :, None, :, None]
    return (shaped * factor).reshape(bands_count, out_size, in_size)


def both_bands(left, operand, band):
    first = jnp.dot(
        left[0], operand, precision=lax.Precision.HIGHEST, preferred_element_type=jnp.float32
    )
    second = jnp.dot(
        left[1], operand, precision=lax.Precision.HIGHEST, preferred_element_type=jnp.float32
    )
    column_mask = jnp.tile(band == 0, 2)
    return jnp.where(column_mask[None, :], first, second)


def local(spectrum, operator, pattern, band):
    moved = lax.all_to_all(spectrum, "lat", split_axis=3, concat_axis=1, tiled=True)
    depth_local = moved.shape[1]
    rows_local = moved.shape[3]
    planes = moved.reshape(depth_local, 2 * rows_local)
    depth_index = lax.axis_index("dep")
    local_blocks = depth_local // BLOCK
    column_pattern = lax.dynamic_slice_in_dim(pattern, depth_index * local_blocks, local_blocks, 2)
    masked = apply_pattern(operator, column_pattern)
    result = lax.psum_scatter(
        both_bands(masked, planes, band), "dep", scatter_dimension=0, tiled=True
    )
    return result.reshape(depth_local, 2, rows_local)


def solution(mesh):
    placed = (P("dep", "lat", None, None), P(None, None, "dep"), P(), P("lat"))
    return jax.shard_map(
        local, mesh=mesh, in_specs=placed, out_specs=P("dep", None, "lat"), check_vma=False
    )
```

profile of v0, /device:TPU:0, one launch (start us, length us, event | category | flops | bytes accessed | tf_op | source)
XLA Modules:
  0.0 492.0 jit_solution(18039659638275920538)
XLA Ops:
  6.5 36.1 %copy.8 = f32[1,16,2,32768]{1,2,0,3:T(2,128)} copy(f32[1,16,2,32768]{3,2,1,0:T(2,128)} %param.4) | data formatting | bytes 8388608 | tf_op args[0]
  42.6 48.6 %reshape.21 = f32[32,1,32768]{2,1,0:T(1,128)} reshape(f32[32768,1,2,16]{3,2,1,0:T(2,128)} %bitcast.20) | data formatting | bytes 8388608
  91.2 7.6 %all-to-all-start = ((f32[32,1,32768]{2,1,0:T(1,128)}), f32[32,1,32768]{2,1,0:T(1,128)}, u32[]{:S(2)}, u32[]{:S(2)}) async-start(f32[32,1,32768]{2,1,0:T(1,128)} %reshape.21), calls=%async_computation | async-start | bytes 8388608 | tf_op jit(solution)/shard_map/all_to_all | solution.py:28
  98.8 0.0 reduce-scatter.2.cloned.1.call-start
  98.8 0.0 copy-start.3
  98.9 0.0 copy-start.2
  98.9 9.9 %reshape.18 = f32[2,16,128,4,128]{4,3,2,1,0:T(4,128)} reshape(f32[2,2048,512]{2,1,0:T(8,128)} %param.5) | data formatting | bytes 16777216 | tf_op jit(solution)/shard_map/reshape | solution.py:11
  108.8 0.0 copy-done.3
  108.8 0.0 copy-done.2
  108.8 0.1 dynamic-slice_convert_fusion
  108.9 9.2 %broadcast_multiply_fusion = f32[2,16,128,4,128]{4,3,2,1,0:T(4,128)} fusion(f32[2,16,128,4,128]{4,3,2,1,0:T(4,128)} %reshape.18, f32[2,16,4]{2,1,0:T(8,128)S(1)} %dynamic-slice_convert_fusion), kind=kLoop, calls=%fused_computation.6 | loop fusion | flops 2097152 | bytes 16777728 | tf_op jit(solution)/shard_map/mul | solution.py:13
  118.1 7.6 %fusion.5 = (f32[1,16,128,4,128]{4,3,2,1,0:T(4,128)}, f32[1,16,128,4,128]{4,3,2,1,0:T(4,128)}) fusion(f32[2,16,128,4,128]{4,3,2,1,0:T(4,128)} %broadcast_multiply_fusion), kind=kLoop, calls=%fused_computation.9 | loop fusion | bytes 16777216 | tf_op jit(solution)/shard_map/slice | solution.py:21
  125.7 25.6 %all-to-all-done = f32[32,1,32768]{2,1,0:T(1,128)} async-done(((f32[32,1,32768]{2,1,0:T(1,128)}), f32[32,1,32768]{2,1,0:T(1,128)}, u32[]{:S(2)}, u32[]{:S(2)}) %all-to-all-start) | async-done | bytes 4194336 | tf_op jit(solution)/shard_map/all_to_all | solution.py:28
  151.3 0.5 broadcast.2
  151.8 13.7 %reduce = f32[32,32768]{1,0:T(8,128)} reduce(f32[32,1,32768]{2,1,0:T(1,128)} %all-to-all-done, f32[]{:T(128)} %broadcast.2), dimensions={1}, to_apply=%all_to_all.11.reduce_sub_computation | reduce | bytes 8388612 | tf_op jit(solution)/shard_map/all_to_all | solution.py:28
  165.5 62.8 %reshape.22 = f32[32768,1,2,16]{3,2,1,0:T(2,128)} reshape(f32[32,32768]{1,0:T(8,128)} %reduce) | data formatting | bytes 8388608
  228.3 38.9 %copy.9 = f32[1,16,2,32,1024]{4,2,1,3,0:T(2,128)} copy(f32[1,16,2,32,1024]{1,2,4,3,0:T(2,128)} %bitcast.19) | data formatting | bytes 8388608 | tf_op jit(solution)/shard_map/all_to_all | solution.py:28
  267.2 0.0 copy-start
  267.2 4.3 copy.11
  271.5 0.0 copy-done
  271.5 0.0 copy-start.1
  271.5 27.2 %fusion.2 = f32[2048,2048]{1,0:T(8,128)S(1)} fusion(f32[512,2048]{1,0:T(8,128)S(1)} %bitcast.21, f32[256,8,4,128]{3,2,1,0:T(4,128)S(1)} %bitcast.23), kind=kOutput, calls=%fused_computation.3 | convolution fusion | flops 25769803776 | bytes 25165824 | tf_op jit(solution)/shard_map/dot_general | solution.py:17
  298.7 0.0 copy-done.1
  298.7 29.8 %broadcast_select_fusion = f32[2048,2048]{1,0:T(8,128)} fusion(f32[2048,2048]{1,0:T(8,128)S(1)} %fusion.2, pred[2048]{0:T(1024)(128)(4,1)S(1)} %broadcast_in_dim.11, f32[512,2048]{1,0:T(8,128)S(1)} %bitcast.22, f32[256,8,4,128]{3,2,1,0:T(4,128)S(1)} %bitcast.25), kind=kOutput, calls=%fused_computation | convolution fusion | flops 25773998080 | bytes 41945088 | tf_op jit(solution)/shard_map/dot_general | solution.py:20
  328.5 0.0 reduce-scatter.2.cloned.1.call-update
  328.6 150.0 %reduce-scatter.2.cloned.1.call-done = f32[512,2048]{1,0:T(8,128)} async-done(((f32[2048,2048]{1,0:T(8,128)}), f32[512,2048]{1,0:T(8,128)}) %reduce-scatter.2.cloned.1.call-update) | async-done | bytes 4194320 | tf_op jit(solution)/shard_map/reduce_scatter | solution.py:36
  478.6 6.6 %reshape.20 = f32[512,2,1024]{2,1,0:T(2,128)} reshape(f32[512,2048]{1,0:T(8,128)} %reduce-scatter.2.cloned.1.call-done) | data formatting | bytes 8388608 | tf_op jit(solution)/shard_map/reshape | solution.py:39
  (3 shorter events, 0.0 us)
Async XLA Ops:
  91.2 60.0 %all-to-all-start = ((f32[32,1,32768]{2,1,0:T(1,128)}), f32[32,1,32768]{2,1,0:T(1,128)}, u32[]{:S(2)}, u32[]{:S(2)}) async-start(f32[32,1,32768]{2,1,0:T(1,128)} %reshape.21), calls=%async_computation | async-start | bytes 8388608 | tf_op jit(solution)/shard_map/all_to_all | solution.py:28
  98.8 379.8 %reduce-scatter.2.cloned.1.call-start = ((), (), s32[]{:S(2)}) async-start(), calls=%async_computation.2 | async-start | bytes 20971520 | tf_op jit(solution)/shard_map/reduce_scatter | solution.py:36
  98.8 9.9 %copy-start.3 = (s32[1024]{0:T(1024)S(1)}, s32[1024]{0:T(1024)}, u32[]{:S(2)}) copy-start(s32[1024]{0:T(1024)} %param.7) | copy-start | bytes 12292
  98.9 10.0 %copy-start.2 = (s32[2,16,16]{2,1,0:T(8,128)S(1)}, s32[2,16,16]{2,1,0:T(8,128)}, u32[]{:S(2)}) copy-start(s32[2,16,16]{2,1,0:T(8,128)} %param.6) | copy-start | bytes 6148
  267.2 4.3 copy-start
  271.5 27.2 %copy-start.1 = (f32[1,16,128,4,128]{4,3,2,1,0:T(4,128)S(1)}, f32[1,16,128,4,128]{4,3,2,1,0:T(4,128)}, u32[]{:S(2)}) copy-start(f32[1,16,128,4,128]{4,3,2,1,0:T(4,128)} %get-tuple-element.5) | copy-start | bytes 12582916
Sparse Core Ops, SparseCore 0:
  328.7 149.8 reduce-scatter.1
where the time goes:
time: 496 us; the launch traced here: 492 us
  local copies, waits for them, and re-layouts  215 us (43%)
  waiting for transfers between devices  176 us (35%)
  matrix products  57 us (11%)
  other arithmetic  23 us (5%)
  between operations  13.5 us (3%)
  starting transfers between devices  7.6 us (2%)
    unnamed x12, local copies, waits for them, and re-layouts  152 us
    reduce_scatter x1, waiting for transfers between devices, local(): lax.psum_scatter(both_bands(masked, planes, band), 'dep', scatter_dimensi...  150 us
    all_to_all x2, local copies, waits for them, and re-layouts, local(): lax.all_to_all(spectrum, 'lat', split_axis=3, concat_axis=1, tiled=True)  39.4 us
    dot_general x1, matrix products, both_bands(): jnp.dot(left[1], operand, precision=lax.Precision.HIGHEST, preferred_elem...  29.8 us
    dot_general x1, matrix products, both_bands(): jnp.dot(left[0], operand, precision=lax.Precision.HIGHEST, preferred_elem...  27.2 us
    all_to_all x1, waiting for transfers between devices, local(): lax.all_to_all(spectrum, 'lat', split_axis=3, concat_axis=1, tiled=True)  25.6 us
    all_to_all x1, other arithmetic, local(): lax.all_to_all(spectrum, 'lat', split_axis=3, concat_axis=1, tiled=True)  13.7 us
  transfers between devices with their start and end apart: 2, of which 2 were waited for; matrix products, arithmetic and copies ran while one was open for 5% of the time, Pallas kernels for 0%

commit v1 on v0

v1 whole, which is shorter than its diff:
```python
import jax
import jax.numpy as jnp
from jax import lax
from jax.sharding import PartitionSpec as P

BLOCK = 128
CHUNKS = 4


def apply_pattern(weights, blocks):
    bands_count, out_size, in_size = weights.shape
    shaped = weights.reshape(bands_count, out_size // BLOCK, BLOCK, in_size // BLOCK, BLOCK)
    factor = blocks.astype(jnp.float32)[:, :, None, :, None]
    return (shaped * factor).reshape(bands_count, out_size, in_size)


def both_bands(left, operand, column_mask):
    first = jnp.dot(
        left[0], operand, precision=lax.Precision.HIGHEST, preferred_element_type=jnp.float32
    )
    second = jnp.dot(
        left[1], operand, precision=lax.Precision.HIGHEST, preferred_element_type=jnp.float32
    )
    return jnp.where(column_mask[None, :], first, second)


def solution(mesh):
    n_lat = mesh.shape["lat"]

    def local(spectrum, operator, pattern, band):
        _, sub, parts, rows = spectrum.shape
        rows_local = rows // n_lat
        cols = parts * rows_local
        send = spectrum.reshape(sub, parts, n_lat, rows_local)
        send = jnp.transpose(send, (2, 0, 1, 3)).reshape(n_lat, sub, cols)
        moved = lax.all_to_all(send, "lat", 0, 0, tiled=True)
        planes = moved.reshape(n_lat * sub, cols)
        depth_local = planes.shape[0]
        depth_index = lax.axis_index("dep")
        local_blocks = depth_local // BLOCK
        column_pattern = lax.dynamic_slice_in_dim(pattern, depth_index * local_blocks, local_blocks, 2)
        masked = apply_pattern(operator, column_pattern)
        column_mask = jnp.tile(band == 0, parts)
        width = cols // CHUNKS
        pieces = []
        for c in range(CHUNKS):
            part = both_bands(
                masked, planes[:, c * width:(c + 1) * width], column_mask[c * width:(c + 1) * width]
            )
            pieces.append(lax.psum_scatter(part, "dep", scatter_dimension=0, tiled=True))
        result = jnp.concatenate(pieces, axis=1)
        return result.reshape(depth_local, parts, rows_local)

    placed = (P("dep", "lat", None, None), P(None, None, "dep"), P(), P("lat"))
    return jax.shard_map(
        local, mesh=mesh, in_specs=placed, out_specs=P("dep", None, "lat"), check_vma=False
    )
```

time: 496 us -> 326 us (0.66)
  local copies, waits for them, and re-layouts: 215 us -> 44.8 us
  matrix products: 57 us -> 74.3 us
  waiting for transfers between devices: 176 us -> 164 us
  other arithmetic: 23 us -> 13.8 us
    unnamed x12, local copies, waits for them, and re-layouts: 152 us -> 0.04 us
    all_to_all x2 -> x0, local copies, waits for them, and re-layouts: 39.4 us -> none  [local(): lax.all_to_all(spectrum, 'lat', split_axis=3, concat_axis=1, tiled=True)]
    reshape x1 -> x4, local copies, waits for them, and re-layouts: 6.57 us -> 27.2 us  [the longest x2 14 us: local(): send = spectrum.reshape(sub, parts, n_lat, rows_local)]
    all_to_all x1 -> x0, other arithmetic: 13.7 us -> none  [local(): lax.all_to_all(spectrum, 'lat', split_axis=3, concat_axis=1, tiled=True)]
    reduce_scatter x1 -> x4, waiting for transfers between devices: 150 us -> 139 us  [local(): lax.psum_scatter(part, 'dep', scatter_dimension=0, tiled=True)]
    dot_general x1 -> x4, matrix products: 27.2 us -> 37.9 us  [both_bands(): jnp.dot(left[0], operand, precision=lax.Precision.HIGHEST, preferred_elem...]
    dot_general x1 -> x4, matrix products: 29.8 us -> 36.4 us  [both_bands(): jnp.dot(left[1], operand, precision=lax.Precision.HIGHEST, preferred_elem...]
  transfers between devices with their start and end apart: 2 -> 5, of which waited for: 2 -> 4; matrix products, arithmetic and copies ran while one was open for 5% -> 26% of each run, Pallas kernels for 0% -> 0%
where the time goes in v1:
time: 326 us; the launch traced here: 320 us
  waiting for transfers between devices  164 us (50%)
  matrix products  74.3 us (23%)
  local copies, waits for them, and re-layouts  44.8 us (14%)
  other arithmetic  13.8 us (4%)
  between operations  13.5 us (4%)
  starting transfers between devices  8.89 us (3%)
    reduce_scatter x4, waiting for transfers between devices, local(): lax.psum_scatter(part, 'dep', scatter_dimension=0, tiled=True)  139 us
    dot_general x4, matrix products, both_bands(): jnp.dot(left[0], operand, precision=lax.Precision.HIGHEST, preferred_elem...  37.9 us
    dot_general x4, matrix products, both_bands(): jnp.dot(left[1], operand, precision=lax.Precision.HIGHEST, preferred_elem...  36.4 us
    all_to_all x1, waiting for transfers between devices, local(): moved = lax.all_to_all(send, 'lat', 0, 0, tiled=True)  24.9 us
    reshape x2, local copies, waits for them, and re-layouts, local(): send = spectrum.reshape(sub, parts, n_lat, rows_local)  14 us
    reshape x1, local copies, waits for them, and re-layouts, apply_pattern(): weights.reshape(bands_count, out_size // BLOCK, BLOCK, in_size // BLOCK,...  9.93 us
    mul x1, other arithmetic, apply_pattern(): return (shaped * factor).reshape(bands_count, out_size, in_size)  9.2 us
    slice x1, local copies, waits for them, and re-layouts, both_bands(): left[0]  7.68 us
  transfers between devices with their start and end apart: 5, of which 4 were waited for; matrix products, arithmetic and copies ran while one was open for 26% of the time, Pallas kernels for 0%

profile of v1, /device:TPU:0, one launch (start us, length us, event | category | flops | bytes accessed | tf_op | source)
XLA Modules:
  0.0 319.7 jit_solution(5652922025233898278)
XLA Ops:
  6.5 6.6 %reshape.27 = f32[16,2,32,1024]{3,2,1,0:T(8,128)} reshape(f32[1,16,2,32768]{3,2,1,0:T(2,128)} %param.4) | data formatting | bytes 8388608 | tf_op jit(solution)/shard_map/reshape | solution.py:34
  13.1 7.4 %copy.49 = f32[16,2,32,1024]{3,1,0,2:T(2,128)} copy(f32[16,2,32,1024]{3,2,1,0:T(8,128)} %reshape.27) | data formatting | bytes 8388608 | tf_op jit(solution)/shard_map/reshape | solution.py:34
  20.5 6.6 %reshape.28 = f32[32,16,2048]{2,1,0:T(8,128)} reshape(f32[32,16,2,1024]{3,2,1,0:T(2,128)} %bitcast.42) | data formatting | bytes 8388608 | tf_op jit(solution)/shard_map/reshape | solution.py:35
  27.1 7.6 %all-to-all-start = ((f32[32,16,2048]{2,1,0:T(8,128)}), f32[32,16,2048]{2,1,0:T(8,128)}, u32[]{:S(2)}, u32[]{:S(2)}) async-start(f32[32,16,2048]{2,1,0:T(8,128)} %reshape.28), calls=%async_computation | async-start | bytes 8388608 | tf_op jit(solution)/shard_map/all_to_all | solution.py:36
  34.7 0.6 reduce-scatter.5.cloned.1.call-start
  35.3 0.0 copy-start.5
  35.3 0.0 copy-start.4
  35.3 9.9 %reshape.26 = f32[2,16,128,4,128]{4,3,2,1,0:T(4,128)} reshape(f32[2,2048,512]{2,1,0:T(8,128)} %param.5) | data formatting | bytes 16777216 | tf_op jit(solution)/shard_map/reshape | solution.py:12
  45.2 0.0 copy-done.5
  45.3 0.0 copy-done.4
  45.3 0.1 dynamic-slice_convert_fusion
  45.4 9.2 %broadcast_multiply_fusion = f32[2,16,128,4,128]{4,3,2,1,0:T(4,128)} fusion(f32[2,16,128,4,128]{4,3,2,1,0:T(4,128)} %reshape.26, f32[2,16,4]{2,1,0:T(8,128)S(1)} %dynamic-slice_convert_fusion), kind=kLoop, calls=%fused_computation.18 | loop fusion | flops 2097152 | bytes 16777728 | tf_op jit(solution)/shard_map/mul | solution.py:14
  54.6 7.7 %fusion.44 = (f32[1,16,128,4,128]{4,3,2,1,0:T(4,128)}, f32[1,16,128,4,128]{4,3,2,1,0:T(4,128)}) fusion(f32[2,16,128,4,128]{4,3,2,1,0:T(4,128)} %broadcast_multiply_fusion), kind=kLoop, calls=%fused_computation.41 | loop fusion | bytes 16777216 | tf_op jit(solution)/shard_map/slice | solution.py:19
  62.3 24.9 %all-to-all-done = f32[32,16,2048]{2,1,0:T(8,128)} async-done(((f32[32,16,2048]{2,1,0:T(8,128)}), f32[32,16,2048]{2,1,0:T(8,128)}, u32[]{:S(2)}, u32[]{:S(2)}) %all-to-all-start) | async-done | bytes 4194336 | tf_op jit(solution)/shard_map/all_to_all | solution.py:36
  87.2 0.0 copy-start
  87.2 9.1 %fusion.6 = f32[2048,512]{1,0:T(8,128)S(1)} fusion(f32[256,8,4,128]{3,2,1,0:T(4,128)} %bitcast.34, f32[512,2048]{1,0:T(8,128)} %bitcast.1), kind=kOutput, calls=%fused_computation.6 | convolution fusion | flops 6442450944 | bytes 9437184 | tf_op jit(solution)/shard_map/dot_general | solution.py:21
  96.3 0.0 copy-done
  96.3 9.5 %fusion.24 = f32[2048,512]{1,0:T(8,128)} fusion(f32[2048,512]{1,0:T(8,128)S(1)} %fusion.6, f32[256,8,4,128]{3,2,1,0:T(4,128)S(1)} %bitcast.38, pred[512]{0:T(512)(128)(4,1)S(1)} %get-tuple-element.7, f32[512,2048]{1,0:T(8,128)} %bitcast.1), kind=kOutput, calls=%fused_computation.27 | convolution fusion | flops 6443499520 | bytes 13632000 | tf_op jit(solution)/shard_map/dot_general | solution.py:18
  105.8 0.0 reduce-scatter.5.cloned.1.call-update
  105.8 0.2 reduce-scatter.7.cloned.1.call-start
  106.0 0.0 copy-start.1
  106.0 9.1 %fusion.4 = f32[2048,512]{1,0:T(8,128)S(1)} fusion(f32[256,8,4,128]{3,2,1,0:T(4,128)} %bitcast.35, f32[512,2048]{1,0:T(8,128)} %bitcast.1), kind=kOutput, calls=%fused_computation.4 | convolution fusion | flops 6442450944 | bytes 9437184 | tf_op jit(solution)/shard_map/dot_general | solution.py:21
  115.2 0.0 copy-done.1
  115.2 9.5 %fusion.27 = f32[2048,512]{1,0:T(8,128)} fusion(f32[2048,512]{1,0:T(8,128)S(1)} %fusion.4, f32[256,8,4,128]{3,2,1,0:T(4,128)S(1)} %bitcast.39, pred[512]{0:T(512)(128)(4,1)S(1)} %get-tuple-element.10, f32[512,2048]{1,0:T(8,128)} %bitcast.1), kind=kOutput, calls=%fused_computation.28 | convolution fusion | flops 6443499520 | bytes 13632000 | tf_op jit(solution)/shard_map/dot_general | solution.py:18
  124.7 0.0 reduce-scatter.7.cloned.1.call-update
  124.7 0.3 reduce-scatter.9.cloned.1.call-start
  125.0 0.0 copy-start.2
  125.0 9.1 %fusion.2 = f32[2048,512]{1,0:T(8,128)S(1)} fusion(f32[256,8,4,128]{3,2,1,0:T(4,128)} %bitcast.36, f32[512,2048]{1,0:T(8,128)} %bitcast.1), kind=kOutput, calls=%fused_computation.2 | convolution fusion | flops 6442450944 | bytes 9437184 | tf_op jit(solution)/shard_map/dot_general | solution.py:21
  134.1 0.0 copy-done.2
  134.1 9.5 %fusion.30 = f32[2048,512]{1,0:T(8,128)} fusion(f32[2048,512]{1,0:T(8,128)S(1)} %fusion.2, f32[256,8,4,128]{3,2,1,0:T(4,128)S(1)} %bitcast.40, pred[512]{0:T(512)(128)(4,1)S(1)} %get-tuple-element.9, f32[512,2048]{1,0:T(8,128)} %bitcast.1), kind=kOutput, calls=%fused_computation.29 | convolution fusion | flops 6443499520 | bytes 13632000 | tf_op jit(solution)/shard_map/dot_general | solution.py:18
  143.6 0.0 reduce-scatter.9.cloned.1.call-update
  143.6 0.3 reduce-scatter.11.cloned.1.call-start
  143.9 0.0 copy-start.3
  143.9 9.1 %fusion = f32[2048,512]{1,0:T(8,128)S(1)} fusion(f32[256,8,4,128]{3,2,1,0:T(4,128)} %bitcast.37, f32[512,2048]{1,0:T(8,128)} %bitcast.1), kind=kOutput, calls=%fused_computation | convolution fusion | flops 6442450944 | bytes 9437184 | tf_op jit(solution)/shard_map/dot_general | solution.py:21
  153.0 0.0 copy-done.3
  153.0 9.4 %fusion.33 = f32[2048,512]{1,0:T(8,128)} fusion(f32[2048,512]{1,0:T(8,128)S(1)} %fusion, f32[256,8,4,128]{3,2,1,0:T(4,128)S(1)} %bitcast.41, pred[512]{0:T(512)(128)(4,1)S(1)} %get-tuple-element.8, f32[512,2048]{1,0:T(8,128)} %bitcast.1), kind=kOutput, calls=%fused_computation.30 | convolution fusion | flops 6443499520 | bytes 13632000 | tf_op jit(solution)/shard_map/dot_general | solution.py:18
  162.4 0.0 reduce-scatter.11.cloned.1.call-update
  162.5 0.0 reduce-scatter.5.cloned.1.call-done
  162.5 41.3 %reduce-scatter.7.cloned.1.call-done = f32[512,512]{1,0:T(8,128)} async-done(((f32[2048,512]{1,0:T(8,128)}), f32[512,512]{1,0:T(8,128)}) %reduce-scatter.7.cloned.1.call-update) | async-done | bytes 1048592 | tf_op jit(solution)/shard_map/reduce_scatter | solution.py:50
  203.7 49.1 %reduce-scatter.9.cloned.1.call-done = f32[512,512]{1,0:T(8,128)} async-done(((f32[2048,512]{1,0:T(8,128)}), f32[512,512]{1,0:T(8,128)}) %reduce-scatter.9.cloned.1.call-update) | async-done | bytes 1048592 | tf_op jit(solution)/shard_map/reduce_scatter | solution.py:50
  252.8 48.9 %reduce-scatter.11.cloned.1.call-done = f32[512,512]{1,0:T(8,128)} async-done(((f32[2048,512]{1,0:T(8,128)}), f32[512,512]{1,0:T(8,128)}) %reduce-scatter.11.cloned.1.call-update) | async-done | bytes 1048592 | tf_op jit(solution)/shard_map/reduce_scatter | solution.py:50
  301.8 4.6 %pad_maximum_fusion = f32[512,2048]{1,0:T(8,128)} fusion(f32[512,512]{1,0:T(8,128)} %reduce-scatter.11.cloned.1.call-done, f32[512,512]{1,0:T(8,128)} %reduce-scatter.9.cloned.1.call-done, f32[512,512]{1,0:T(8,128)} %reduce-scatter.7.cloned.1.call-done, f32[512,512]{1,0:T(8,128)} %reduce-scatter.5.cloned.1.call-done), kind=kLoop, calls=%fused_computation.16 | loop fusion | flops 3145728 | bytes 8388608 | tf_op jit(solution)/shard_map/concatenate | solution.py:51
  306.3 6.6 %reshape.30 = f32[512,2,1024]{2,1,0:T(2,128)} reshape(f32[512,2048]{1,0:T(8,128)} %pad_maximum_fusion) | data formatting | bytes 8388608 | tf_op jit(solution)/shard_map/reshape | solution.py:52
  (4 shorter events, 0.0 us)
Async XLA Ops:
  27.1 60.0 %all-to-all-start = ((f32[32,16,2048]{2,1,0:T(8,128)}), f32[32,16,2048]{2,1,0:T(8,128)}, u32[]{:S(2)}, u32[]{:S(2)}) async-start(f32[32,16,2048]{2,1,0:T(8,128)} %reshape.28), calls=%async_computation | async-start | bytes 8388608 | tf_op jit(solution)/shard_map/all_to_all | solution.py:36
  34.7 127.8 %reduce-scatter.5.cloned.1.call-start = ((), (), s32[]{:S(2)}) async-start(), calls=%async_computation.5 | async-start | bytes 5242880 | tf_op jit(solution)/shard_map/reduce_scatter | solution.py:50
  35.3 10.0 %copy-start.5 = (s32[1024]{0:T(1024)S(1)}, s32[1024]{0:T(1024)}, u32[]{:S(2)}) copy-start(s32[1024]{0:T(1024)} %param.7) | copy-start | bytes 12292
  35.3 10.0 %copy-start.4 = (s32[2,16,16]{2,1,0:T(8,128)S(1)}, s32[2,16,16]{2,1,0:T(8,128)}, u32[]{:S(2)}) copy-start(s32[2,16,16]{2,1,0:T(8,128)} %param.6) | copy-start | bytes 6148
  87.2 9.1 %copy-start = (f32[1,16,128,4,128]{4,3,2,1,0:T(4,128)S(1)}, f32[1,16,128,4,128]{4,3,2,1,0:T(4,128)}, u32[]{:S(2)}) copy-start(f32[1,16,128,4,128]{4,3,2,1,0:T(4,128)} %get-tuple-element.5) | copy-start | bytes 12582916
  105.8 97.9 %reduce-scatter.7.cloned.1.call-start = ((), (), s32[]{:S(2)}) async-start(), calls=%async_computation.6 | async-start | bytes 5242880 | tf_op jit(solution)/shard_map/reduce_scatter | solution.py:50
  106.0 9.1 %copy-start.1 = (f32[1,16,128,4,128]{4,3,2,1,0:T(4,128)S(1)}, f32[1,16,128,4,128]{4,3,2,1,0:T(4,128)}, u32[]{:S(2)}) copy-start(f32[1,16,128,4,128]{4,3,2,1,0:T(4,128)} %get-tuple-element.5) | copy-start | bytes 12582916
  124.7 128.1 %reduce-scatter.9.cloned.1.call-start = ((), (), s32[]{:S(2)}) async-start(), calls=%async_computation.7 | async-start | bytes 5242880 | tf_op jit(solution)/shard_map/reduce_scatter | solution.py:50
  125.0 9.1 %copy-start.2 = (f32[1,16,128,4,128]{4,3,2,1,0:T(4,128)S(1)}, f32[1,16,128,4,128]{4,3,2,1,0:T(4,128)}, u32[]{:S(2)}) copy-start(f32[1,16,128,4,128]{4,3,2,1,0:T(4,128)} %get-tuple-element.5) | copy-start | bytes 12582916
  143.6 158.2 %reduce-scatter.11.cloned.1.call-start = ((), (), s32[]{:S(2)}) async-start(), calls=%async_computation.8 | async-start | bytes 5242880 | tf_op jit(solution)/shard_map/reduce_scatter | solution.py:50
  143.9 9.1 %copy-start.3 = (f32[1,16,128,4,128]{4,3,2,1,0:T(4,128)S(1)}, f32[1,16,128,4,128]{4,3,2,1,0:T(4,128)}, u32[]{:S(2)}) copy-start(f32[1,16,128,4,128]{4,3,2,1,0:T(4,128)} %get-tuple-element.5) | copy-start | bytes 12582916
Sparse Core Ops, SparseCore 0:
  105.9 48.7 reduce-scatter.4
  157.1 46.6 reduce-scatter.6
  206.2 46.6 reduce-scatter.8
  255.1 46.6 reduce-scatter.10
